TPU v7x, 128 devices: a whole 4x4x4 slice. The times are simulated.
128 devices in a mesh: dom: 32 (over y, x, core), band: 4 (over z).
Axes of the slice: x: 4, y: 4, z: 4, core: 2. Of those that a mesh axis runs over, the one named last changes fastest.
Arguments:
- states: bfloat16 [256, 393216], P('band', 'dom'), may hold values from -640 to 640
- cell_kinetic: bfloat16 [512, 512], replicated, may hold values from -0.3 to 0.3, as said below
- cell_scale: float32 [1024], P('dom'), may hold values from 0.5 to 2
- cell_potential: float32 [1024, 512], P('dom'), may hold values from -0.3 to 0.3
- connectivity: int32 [1024, 512], P('dom'), may hold values from 0 to 12287, as said below
- shared_nodes: int32 [32, 2, 1024], P('dom'), may hold values from 0 to 12287, as said below
- cell_counts: int32 [32], P('dom'), may hold values from 4 to 32, as said below
Outputs:
- rotated: bfloat16 [256, 393216], P('band', 'dom')
Inputs may be any that keep to these rules, and one draw needn't show every extreme that they name: cell_kinetic is symmetric. `connectivity`: row c of a domain (local cell number c) names each of the 512 nodes c * 3 * 128 to c * 3 * 128 + 511, counted round modulo 12288, exactly once. `shared_nodes`: the two rows of a domain name 2048 distinct nodes; position p of domain d's row 1 and of domain d+1's row 0 are the same physical node. `cell_counts`: in every draw some domain has all 32 cells live.
All inputs are finite; a program needn't handle non-finite values.
Results may differ from a plain program's by a relative error of at most 0.008.
Values may be sent and summed in bfloat16 or wider, within the bound.
No kernel may reach another device: no remote copies, remote signals or barrier semaphores. Data moves between devices by JAX's collectives and lax.ppermute only.
A program may use at most 128 MiB of HBM per device.

v0:
```python
import jax
import jax.numpy as jnp
from jax import lax
from jax.sharding import PartitionSpec as P

CHEB = 4
NS_ITERS = 5


def with_halo(x, sides, width):
    for axis, dim in sides:
        size, length = (lax.axis_size(axis), x.shape[dim])
        up = [(i, (i + 1) % size) for i in range(size - 1)]
        down = [(j, i) for i, j in up]
        last = lax.slice_in_dim(x, length - width, length, axis=dim)
        first = lax.slice_in_dim(x, 0, width, axis=dim)
        before = lax.ppermute(last, axis, up)
        after = lax.ppermute(first, axis, down)
        x = jnp.concatenate([before, x, after], axis=dim)
    return x


def window_operators(connectivity, cell_kinetic, cell_potential, node_total):
    cell_total = connectivity.shape[0]
    width = connectivity.shape[1]
    quarter = width // 4
    starts = jnp.arange(cell_total, dtype=jnp.int32) * (3 * quarter)
    slots = (connectivity - starts[:, None]) % node_total
    onehot = (slots[:, :, None] == jnp.arange(width, dtype=jnp.int32)[None, None, :]).astype(
        jnp.bfloat16
    )
    kinetic_cols = jnp.einsum(
        "ij,cia->cja", cell_kinetic, onehot, preferred_element_type=jnp.float32
    ).astype(jnp.bfloat16)
    window_ops = jnp.einsum(
        "cjb,cja->cba", onehot, kinetic_cols, preferred_element_type=jnp.float32
    ).astype(jnp.bfloat16)
    window_pot = jnp.einsum(
        "ci,cia->ca", cell_potential, onehot.astype(jnp.float32), precision=lax.Precision.HIGHEST
    )
    return (window_ops, window_pot)


def window_terms(windows, window_ops, scales, window_pot, alive_mask):
    product = jnp.einsum("scb,cba->sca", windows, window_ops, preferred_element_type=jnp.float32)
    return (
        product * scales[None, :, None] + window_pot[None] * windows.astype(jnp.float32)
    ) * alive_mask[None, :, None]


def local_apply(vector, window_ops, window_pot, scales, live_count):
    state_rows, node_total = vector.shape
    cell_total, width = window_pot.shape
    quarter = width // 4
    blocked = vector.reshape(state_rows, cell_total, 3, quarter)
    following = jnp.roll(blocked[:, :, 0], -1, axis=1)
    windows = jnp.concatenate([blocked, following[:, :, None]], axis=2).reshape(
        state_rows, cell_total, width
    )
    alive_mask = (jnp.arange(cell_total) < live_count).astype(jnp.float32)
    terms = window_terms(windows, window_ops, scales, window_pot, alive_mask)
    split_terms = terms.reshape(state_rows, cell_total, 4, quarter)
    folded = split_terms[:, :, :3]
    folded = folded.at[:, :, 0].add(jnp.roll(split_terms[:, :, 3], 1, axis=1))
    return folded.reshape(state_rows, node_total)


def newton(gram_matrix):
    identity = jnp.eye(gram_matrix.shape[0], dtype=jnp.float32)
    frobenius = jnp.sqrt(jnp.sum(gram_matrix * gram_matrix))
    scaled = gram_matrix / frobenius
    inverse_root = identity
    for repeat in range(NS_ITERS):
        factor = 1.5 * identity - 0.5 * jnp.dot(
            inverse_root, scaled, precision=lax.Precision.HIGHEST
        )
        scaled = jnp.dot(scaled, factor, precision=lax.Precision.HIGHEST)
        inverse_root = jnp.dot(factor, inverse_root, precision=lax.Precision.HIGHEST)
    return inverse_root.astype(jnp.bfloat16)


def body(states, cell_kinetic, cell_scale, cell_potential, connectivity, shared_nodes, cell_counts):
    left_face = shared_nodes[0, 0]
    right_face = shared_nodes[0, 1]
    live_count = cell_counts[0]
    domain = lax.axis_index("dom")
    domains = lax.axis_size("dom")
    node_total = states.shape[1]
    has_left = (domain > 0).astype(jnp.float32)
    has_right = (domain < domains - 1).astype(jnp.float32)
    multiplicity = (
        jnp.ones((node_total,), jnp.float32)
        .at[left_face]
        .add(has_left)
        .at[right_face]
        .add(has_right)
    )
    node_weight = (1.0 / multiplicity).astype(jnp.bfloat16)
    window_ops, window_pot = window_operators(
        connectivity, cell_kinetic, cell_potential, node_total
    )

    def apply_field(vector):
        local_sum = local_apply(vector, window_ops, window_pot, cell_scale, live_count)
        face_values = jnp.stack([local_sum[:, left_face], local_sum[:, right_face]], axis=1)
        padded = with_halo(face_values, (("dom", 1),), 1)
        return local_sum.at[:, left_face].add(padded[:, 0]).at[:, right_face].add(padded[:, 3])

    previous = states
    current = apply_field(states).astype(jnp.bfloat16)
    for repeat in range(CHEB - 1):
        following = (2.0 * apply_field(current) - previous.astype(jnp.float32)).astype(jnp.bfloat16)
        previous = current
        current = following
    row_shard = lax.all_to_all(current, "band", split_axis=1, concat_axis=0, tiled=True)
    piece_nodes = row_shard.shape[1]
    weight_rows = lax.dynamic_slice_in_dim(
        node_weight, lax.axis_index("band") * piece_nodes, piece_nodes, 0
    )
    weighted = row_shard * weight_rows[None]
    partial_gram = lax.dot_general(
        weighted, row_shard, (((1,), (1,)), ((), ())), preferred_element_type=jnp.float32
    )
    gram_matrix = lax.psum(partial_gram, ("dom", "band"))
    mixing = newton(gram_matrix)
    rotated = lax.dot_general(
        mixing, row_shard, (((0,), (0,)), ((), ())), preferred_element_type=jnp.float32
    ).astype(jnp.bfloat16)
    return lax.all_to_all(rotated, "band", split_axis=0, concat_axis=1, tiled=True)


def solution(mesh):
    in_specs = (
        P("band", "dom"),
        P(),
        P("dom"),
        P("dom", None),
        P("dom", None),
        P("dom", None, None),
        P("dom"),
    )
    out_specs = P("band", "dom")
    return jax.shard_map(body, mesh=mesh, in_specs=in_specs, out_specs=out_specs, check_vma=False)
```

profile of v0, /device:TPU:6, one launch (start us, length us, event | category | flops | bytes accessed | tf_op | source)
XLA Modules:
  0.0 739.6 jit_solution(7477544491735769131)
XLA Ops:
  11.7 8.4 %iota_compare_fusion.21 = pred[32,512,512]{1,2,0:T(32,128)(4,1)} fusion(s32[32,512]{1,0:T(8,128)S(1)} %add_select_fusion), kind=kLoop, calls=%fused_computation.18.clone.1.clone.clone.clone.2 | loop fusion | flops 8388608 | bytes 8454144 | tf_op jit(solution)/shard_map/cjb,cja->cba/dot_general | solution.py:35
  27.6 14.8 %fusion = f32[32,1,512]{2,1,0:T(1,128)S(1)} fusion(s32[32,512]{1,0:T(8,128)S(1)} %add_select_fusion, f32[32,512,1]{1,0,2:T(8,128)S(1)} %bitcast.287), kind=kOutput, calls=%fused_computation.19 | convolution fusion | flops 109051904 | bytes 196608 | tf_op jit(solution)/shard_map/ci,cia->ca/dot_general | solution.py:38
  43.1 22.0 %fusion.7 = bf16[32,512,512]{2,1,0:T(8,128)(2,1)} fusion(s32[32,512]{1,0:T(8,128)S(1)} %add_select_fusion, bf16[512,512]{1,0:T(8,128)(2,1)S(1)} %copy-done, pred[32,512,512]{1,2,0:T(32,128)(4,1)} %iota_compare_fusion.21), kind=kOutput, calls=%fused_computation.25 | convolution fusion | flops 17205035008 | bytes 25755648 | tf_op jit(solution)/shard_map/cjb,cja->cba/dot_general | solution.py:35
  65.1 13.4 %fusion.13 = f32[64,32,512]{2,0,1:T(8,128)} fusion(bf16[32,512,512]{2,1,0:T(8,128)(2,1)} %fusion.7, bf16[64,32,512]{2,1,0:T(8,128)(2,1)S(1)} %reshape.436, f32[32]{0:T(128)S(1)} %compare_convert_fusion, f32[32,512]{1,0:T(8,128)S(1)} %bitcast.240, f32[32]{0:T(128)S(1)} %copy-done.6), kind=kOutput, calls=%fused_computation.36 | convolution fusion | flops 1078984704 | bytes 23134464 | tf_op jit(solution)/shard_map/scb,cba->sca/dot_general | solution.py:45
  83.9 5.7 fusion.51
  89.9 26.4 %scatter-add.90 = f32[64,32,3,128]{3,2,0,1:T(4,128)} dynamic-update-slice(f32[64,32,3,128]{3,2,0,1:T(4,128)} %bitcast.226, f32[64,32,1,128]{3,2,0,1:T(1,128)S(1)} %bitcast.244, s32[]{:T(128)} %constant.118.clone.1, s32[]{:T(128)} %constant.118.clone.1, s32[]{:T(128)} %constant.118.clone.1, s32[]{:T(128)} %constant.118.clone.1) | dynamic-update-slice | bytes 2097156 | tf_op jit(solution)/shard_map/scatter-add | solution.py:64
  116.3 6.9 copy.60
  140.0 10.9 %scatter_custom_fusion = f32[64,12288]{0,1:T(8,128)} fusion(f32[64,12288]{0,1:T(8,128)} %bitcast.214, s32[1024]{0:T(1024)S(1)} %bitcast.282, f32[64,1,1024]{0,2,1:T(8,128)S(1)} %collective-permute-done), kind=kCustom, calls=%fused_computation.82 | custom fusion | flops 65536 | bytes 3670016 | tf_op jit(solution)/shard_map/scatter-add | solution.py:107
  150.9 10.9 %scatter_custom_fusion.1 = f32[64,12288]{0,1:T(8,128)} fusion(f32[64,12288]{0,1:T(8,128)} %scatter_custom_fusion, s32[1024]{0:T(1024)S(1)} %bitcast.276, f32[64,1,1024]{0,2,1:T(8,128)S(1)} %collective-permute-done.1), kind=kCustom, calls=%fused_computation.80 | custom fusion | flops 65536 | bytes 3670016 | tf_op jit(solution)/shard_map/scatter-add | solution.py:107
  180.1 10.5 %fusion.12 = f32[64,32,512]{2,0,1:T(8,128)} fusion(bf16[64,32,512]{2,0,1:T(8,128)(2,1)S(1)} %reshape.275, bf16[32,512,512]{2,1,0:T(8,128)(2,1)} %fusion.7, f32[32]{0:T(128)S(1)} %compare_convert_fusion, f32[32,512]{1,0:T(8,128)S(1)} %bitcast.241, f32[32]{0:T(128)S(1)} %copy-done.6), kind=kOutput, calls=%fused_computation.34 | convolution fusion | flops 1078984704 | bytes 23134464 | tf_op jit(solution)/shard_map/scb,cba->sca/dot_general | solution.py:45
  195.9 5.7 fusion.50
  201.9 26.4 %scatter-add.93 = f32[64,32,3,128]{3,2,0,1:T(4,128)} dynamic-update-slice(f32[64,32,3,128]{3,2,0,1:T(4,128)} %bitcast.227, f32[64,32,1,128]{3,2,0,1:T(1,128)S(1)} %bitcast.245, s32[]{:T(128)} %constant.118.clone.1, s32[]{:T(128)} %constant.118.clone.1, s32[]{:T(128)} %constant.118.clone.1, s32[]{:T(128)} %constant.118.clone.1) | dynamic-update-slice | bytes 2097156 | tf_op jit(solution)/shard_map/scatter-add | solution.py:64
  228.3 6.9 copy.66
  235.2 6.9 gather_fusion.2
  258.4 10.9 %scatter_custom_fusion.2 = f32[64,12288]{0,1:T(8,128)} fusion(f32[64,12288]{0,1:T(8,128)} %bitcast.220, s32[1024]{0:T(1024)S(1)} %bitcast.283, f32[64,1,1024]{0,2,1:T(8,128)S(1)} %collective-permute-done.2), kind=kCustom, calls=%fused_computation.78 | custom fusion | flops 65536 | bytes 3670016 | tf_op jit(solution)/shard_map/scatter-add | solution.py:107
  269.3 10.9 %scatter_custom_fusion.3 = f32[64,12288]{0,1:T(8,128)} fusion(f32[64,12288]{0,1:T(8,128)} %scatter_custom_fusion.2, s32[1024]{0:T(1024)S(1)} %bitcast.277, f32[64,1,1024]{0,2,1:T(8,128)S(1)} %collective-permute-done.3), kind=kCustom, calls=%fused_computation.76 | custom fusion | flops 65536 | bytes 3670016 | tf_op jit(solution)/shard_map/scatter-add | solution.py:107
  299.9 10.5 %fusion.11 = f32[64,32,512]{2,0,1:T(8,128)} fusion(bf16[64,32,512]{2,0,1:T(8,128)(2,1)S(1)} %reshape.280, bf16[32,512,512]{2,1,0:T(8,128)(2,1)} %fusion.7, f32[32]{0:T(128)S(1)} %compare_convert_fusion, f32[32,512]{1,0:T(8,128)S(1)} %bitcast.242, f32[32]{0:T(128)S(1)} %copy-done.6), kind=kOutput, calls=%fused_computation.32 | convolution fusion | flops 1078984704 | bytes 23134464 | tf_op jit(solution)/shard_map/scb,cba->sca/dot_general | solution.py:45
  315.6 5.7 fusion.49
  321.6 26.4 %scatter-add.96 = f32[64,32,3,128]{3,2,0,1:T(4,128)} dynamic-update-slice(f32[64,32,3,128]{3,2,0,1:T(4,128)} %bitcast.228, f32[64,32,1,128]{3,2,0,1:T(1,128)S(1)} %bitcast.246, s32[]{:T(128)} %constant.118.clone.1, s32[]{:T(128)} %constant.118.clone.1, s32[]{:T(128)} %constant.118.clone.1, s32[]{:T(128)} %constant.118.clone.1) | dynamic-update-slice | bytes 2097156 | tf_op jit(solution)/shard_map/scatter-add | solution.py:64
  348.0 6.9 copy.73
  376.6 11.0 %scatter_custom_fusion.4 = f32[64,12288]{0,1:T(8,128)} fusion(f32[64,12288]{0,1:T(8,128)} %bitcast.223, s32[1024]{0:T(1024)S(1)} %bitcast.284, f32[64,1,1024]{0,2,1:T(8,128)S(1)} %collective-permute-done.4), kind=kCustom, calls=%fused_computation.74 | custom fusion | flops 65536 | bytes 3670016 | tf_op jit(solution)/shard_map/scatter-add | solution.py:107
  387.7 10.9 %scatter_custom_fusion.5 = f32[64,12288]{0,1:T(8,128)} fusion(f32[64,12288]{0,1:T(8,128)} %scatter_custom_fusion.4, s32[1024]{0:T(1024)S(1)} %bitcast.278, f32[64,1,1024]{0,2,1:T(8,128)S(1)} %collective-permute-done.5), kind=kCustom, calls=%fused_computation.72 | custom fusion | flops 65536 | bytes 3670016 | tf_op jit(solution)/shard_map/scatter-add | solution.py:107
  418.7 10.5 %fusion.10 = f32[64,32,512]{2,0,1:T(8,128)} fusion(bf16[64,32,512]{2,0,1:T(8,128)(2,1)S(1)} %reshape.285, bf16[32,512,512]{2,1,0:T(8,128)(2,1)} %fusion.7, f32[32]{0:T(128)S(1)} %compare_convert_fusion, f32[32,512]{1,0:T(8,128)S(1)} %bitcast.243, f32[32]{0:T(128)S(1)} %copy-done.6), kind=kOutput, calls=%fused_computation.30 | convolution fusion | flops 1078984704 | bytes 23134464 | tf_op jit(solution)/shard_map/scb,cba->sca/dot_general | solution.py:45
  434.4 5.7 fusion.48
  440.4 26.4 %scatter-add.99 = f32[64,32,3,128]{3,2,0,1:T(4,128)} dynamic-update-slice(f32[64,32,3,128]{3,2,0,1:T(4,128)} %bitcast.229, f32[64,32,1,128]{3,2,0,1:T(1,128)S(1)} %bitcast.247, s32[]{:T(128)} %constant.118.clone.1, s32[]{:T(128)} %constant.118.clone.1, s32[]{:T(128)} %constant.118.clone.1, s32[]{:T(128)} %constant.118.clone.1) | dynamic-update-slice | bytes 2097156 | tf_op jit(solution)/shard_map/scatter-add | solution.py:64
  466.8 6.9 copy.79
  495.4 11.1 %scatter_custom_fusion.6 = f32[64,12288]{0,1:T(8,128)} fusion(f32[64,12288]{0,1:T(8,128)} %bitcast.217, s32[1024]{0:T(1024)S(1)} %bitcast.285, f32[64,1,1024]{0,2,1:T(8,128)S(1)} %collective-permute-done.6), kind=kCustom, calls=%fused_computation.70 | custom fusion | flops 65536 | bytes 3670016 | tf_op jit(solution)/shard_map/scatter-add | solution.py:107
  506.5 10.9 %scatter_custom_fusion.7 = f32[64,12288]{0,1:T(8,128)} fusion(f32[64,12288]{0,1:T(8,128)} %scatter_custom_fusion.6, s32[1024]{0:T(1024)S(1)} %bitcast.279, f32[64,1,1024]{0,2,1:T(8,128)S(1)} %collective-permute-done.7), kind=kCustom, calls=%fused_computation.68 | custom fusion | flops 65536 | bytes 3670016 | tf_op jit(solution)/shard_map/scatter-add | solution.py:107
  532.4 5.9 scatter_custom_fusion.8
  538.3 6.3 scatter_fusion
  551.7 144.9 %all-reduce.2.cloned.1.call-done = f32[256,256]{1,0:T(8,128)} async-done(((f32[256,256]{1,0:T(8,128)}), f32[256,256]{1,0:T(8,128)}) %all-reduce.2.cloned.1.call-update) | async-done | bytes 262160 | tf_op jit(solution)/shard_map/psum | solution.py:124
  706.8 24.2 %all_to_all.38 = bf16[4,64,3072]{2,1,0:T(8,128)(2,1)S(1)} all-to-all(bf16[4,64,3072]{2,1,0:T(8,128)(2,1)S(1)} %bitcast.237), channel_id=1, replica_groups=mesh['dom'=32,'band'=4] {'band'}, dimensions={0} | all-to-all | bytes 3145728 | tf_op jit(solution)/shard_map/all_to_all | solution.py:129
  (134 shorter events, 201.8 us)
Async XLA Ops:
  6.5 36.5 %copy-start = (bf16[512,512]{1,0:T(8,128)(2,1)S(1)}, bf16[512,512]{1,0:T(8,128)(2,1)}, u32[]{:S(2)}) copy-start(bf16[512,512]{1,0:T(8,128)(2,1)} %param.16) | copy-start | bytes 1572868
  6.5 5.1 copy-start.7
  21.4 6.2 copy-start.9
  43.1 22.0 %copy-start.6 = (f32[32]{0:T(128)S(1)}, f32[32]{0:T(128)}, u32[]{:S(2)}) copy-start(f32[32]{0:T(128)} %param.17) | copy-start | bytes 388
  116.3 6.9 copy-start.8
  128.8 11.2 %collective-permute-start = (f32[64,1,1024]{0,2,1:T(8,128)S(1)}, f32[64,1,1024]{0,2,1:T(8,128)S(1)}, u32[]{:S(2)}, u32[]{:S(2)}) collective-permute-start(f32[64,1,1024]{0,2,1:T(8,128)S(1)} %bitcast.271), channel_id=1, source_target_pairs={{0,4},{4,8},{8,12},{12,16},{16,20},{20,24},{24,28},{28,32},{32,36}... | collective-permute-start | bytes 786440 | tf_op jit(solution)/shard_map/ppermute | solution.py:17
  136.4 14.6 %collective-permute-start.1 = (f32[64,1,1024]{0,2,1:T(8,128)S(1)}, f32[64,1,1024]{0,2,1:T(8,128)S(1)}, u32[]{:S(2)}, u32[]{:S(2)}) collective-permute-start(f32[64,1,1024]{0,2,1:T(8,128)S(1)} %bitcast.272), channel_id=1, source_target_pairs={{4,0},{8,4},{12,8},{16,12},{20,16},{24,20},{28,24},{32,28},{36,32}... | collective-permute-start | bytes 786440 | tf_op jit(solution)/shard_map/ppermute | solution.py:18
  165.1 1.7 copy-start.3
  235.2 18.1 %copy-start.5 = (bf16[64,12288]{1,0:T(8,128)(2,1)S(1)}, bf16[64,12288]{1,0:T(8,128)(2,1)}, u32[]{:S(2)}) copy-start(bf16[64,12288]{1,0:T(8,128)(2,1)} %param.15) | copy-start | bytes 4718596
  247.7 10.7 %collective-permute-start.2 = (f32[64,1,1024]{0,2,1:T(8,128)}, f32[64,1,1024]{0,2,1:T(8,128)S(1)}, u32[]{:S(2)}, u32[]{:S(2)}) collective-permute-start(f32[64,1,1024]{0,2,1:T(8,128)} %bitcast.31), channel_id=1, source_target_pairs={{0,4},{4,8},{8,12},{12,16},{16,20},{20,24},{24,28},{28,32},{32,36}... | collective-permute-start | bytes 786440 | tf_op jit(solution)/shard_map/ppermute | solution.py:17
  249.7 19.7 %collective-permute-start.3 = (f32[64,1,1024]{0,2,1:T(8,128)S(1)}, f32[64,1,1024]{0,2,1:T(8,128)S(1)}, u32[]{:S(2)}, u32[]{:S(2)}) collective-permute-start(f32[64,1,1024]{0,2,1:T(8,128)S(1)} %bitcast.268), channel_id=1, source_target_pairs={{4,0},{8,4},{12,8},{16,12},{20,16},{24,20},{28,24},{32,28},{36,32}... | collective-permute-start | bytes 786440 | tf_op jit(solution)/shard_map/ppermute | solution.py:18
  284.9 1.6 copy-start.2
  366.1 10.5 %collective-permute-start.4 = (f32[64,1,1024]{0,2,1:T(8,128)S(1)}, f32[64,1,1024]{0,2,1:T(8,128)S(1)}, u32[]{:S(2)}, u32[]{:S(2)}) collective-permute-start(f32[64,1,1024]{0,2,1:T(8,128)S(1)} %bitcast.274), channel_id=1, source_target_pairs={{0,4},{4,8},{8,12},{12,16},{16,20},{20,24},{24,28},{28,32},{32,36}... | collective-permute-start | bytes 786440 | tf_op jit(solution)/shard_map/ppermute | solution.py:17
  369.4 18.3 %collective-permute-start.5 = (f32[64,1,1024]{0,2,1:T(8,128)S(1)}, f32[64,1,1024]{0,2,1:T(8,128)S(1)}, u32[]{:S(2)}, u32[]{:S(2)}) collective-permute-start(f32[64,1,1024]{0,2,1:T(8,128)S(1)} %bitcast.270), channel_id=1, source_target_pairs={{4,0},{8,4},{12,8},{16,12},{20,16},{24,20},{28,24},{32,28},{36,32}... | collective-permute-start | bytes 786440 | tf_op jit(solution)/shard_map/ppermute | solution.py:18
  403.6 1.7 copy-start.4
  484.9 10.5 %collective-permute-start.6 = (f32[64,1,1024]{0,2,1:T(8,128)S(1)}, f32[64,1,1024]{0,2,1:T(8,128)S(1)}, u32[]{:S(2)}, u32[]{:S(2)}) collective-permute-start(f32[64,1,1024]{0,2,1:T(8,128)S(1)} %bitcast.273), channel_id=1, source_target_pairs={{0,4},{4,8},{8,12},{12,16},{16,20},{20,24},{24,28},{28,32},{32,36}... | collective-permute-start | bytes 786440 | tf_op jit(solution)/shard_map/ppermute | solution.py:17
  490.2 16.3 %collective-permute-start.7 = (f32[64,1,1024]{0,2,1:T(8,128)S(1)}, f32[64,1,1024]{0,2,1:T(8,128)S(1)}, u32[]{:S(2)}, u32[]{:S(2)}) collective-permute-start(f32[64,1,1024]{0,2,1:T(8,128)S(1)} %bitcast.269), channel_id=1, source_target_pairs={{4,0},{8,4},{12,8},{16,12},{20,16},{24,20},{28,24},{32,28},{36,32}... | collective-permute-start | bytes 786440 | tf_op jit(solution)/shard_map/ppermute | solution.py:18
  527.1 23.2 %all-to-all-start = ((bf16[64,4,3072]{2,0,1:T(8,128)(2,1)}), bf16[64,4,3072]{2,0,1:T(8,128)(2,1)S(1)}, u32[]{:S(2)}, u32[]{:S(2)}) async-start(bf16[64,4,3072]{2,0,1:T(8,128)(2,1)} %copy.80), calls=%async_computation | async-start | bytes 3145728 | tf_op jit(solution)/shard_map/all_to_all | solution.py:115
  532.4 164.3 %all-reduce.2.cloned.1.call-start = ((), (), s32[]{:S(2)}) async-start(), calls=%async_computation.2 | async-start | bytes 524288 | tf_op jit(solution)/shard_map/psum | solution.py:124
  705.8 26.5 %copy-start.1 = (bf16[512,512]{1,0:T(8,128)(2,1)S(1)}, bf16[512,512]{1,0:T(8,128)(2,1)}, u32[]{:S(2)}) copy-start(bf16[512,512]{1,0:T(8,128)(2,1)} %param.16) | copy-start | bytes 1572868
Sparse Core Ops, SparseCore 0:
  551.9 144.7 all-reduce.1
where the time goes:
time: 753 us; the launch traced here: 740 us
  local copies, waits for them, and re-layouts  276 us (37%)
  waiting for transfers between devices  161 us (21%)
  other arithmetic  142 us (19%)
  matrix products  90.7 us (12%)
  starting transfers between devices  29.2 us (4%)
  blocking collectives  24.2 us (3%)
  between operations  16 us (2%)
    psum x1, waiting for transfers between devices, body(): gram_matrix = lax.psum(partial_gram, ('dom', 'band'))  145 us
    scatter-add x8, local copies, waits for them, and re-layouts, local_apply(): folded = folded.at[:, :, 0].add(jnp.roll(split_terms[:, :, 3], 1, axis=1))  133 us
    scatter-add x8, other arithmetic, apply_field(): local_sum.at[:, left_face].add(padded[:, 0]).at[:, right_face]  87.5 us
    dot_general x4, matrix products, window_terms(): jnp.einsum('scb,cba->sca', windows, window_ops, preferred_element_type=jn...  44.9 us
    all_to_all x1, blocking collectives, body(): lax.all_to_all(rotated, 'band', split_axis=0, concat_axis=1, tiled=True)  24.2 us
    gather x4, local copies, waits for them, and re-layouts, apply_field(): local_sum[:, right_face]  23.7 us
    slice x12, local copies, waits for them, and re-layouts, local_apply(): folded = folded.at[:, :, 0].add(jnp.roll(split_terms[:, :, 3], 1, axis=1))  23.2 us
    gather x4, local copies, waits for them, and re-layouts, apply_field(): local_sum[:, left_face]  22.4 us
  transfers between devices with their start and end apart: 10, of which 5 were waited for; matrix products, arithmetic and copies ran while one was open for 9% of the time, Pallas kernels for 0%

commit v1 on v0

v1 whole, which is shorter than its diff:
```python
import jax
import jax.numpy as jnp
from jax import lax
from jax.sharding import PartitionSpec as P

CHEB = 4
NS_ITERS = 5


def window_operators(connectivity, cell_kinetic, cell_potential, node_total):
    cell_total = connectivity.shape[0]
    width = connectivity.shape[1]
    quarter = width // 4
    starts = jnp.arange(cell_total, dtype=jnp.int32) * (3 * quarter)
    slots = (connectivity - starts[:, None]) % node_total
    onehot = (slots[:, :, None] == jnp.arange(width, dtype=jnp.int32)[None, None, :]).astype(
        jnp.bfloat16
    )
    kinetic_cols = jnp.einsum(
        "ij,cia->cja", cell_kinetic, onehot, preferred_element_type=jnp.float32
    ).astype(jnp.bfloat16)
    window_ops = jnp.einsum(
        "cjb,cja->cba", onehot, kinetic_cols, preferred_element_type=jnp.float32
    ).astype(jnp.bfloat16)
    window_pot = jnp.einsum(
        "ci,cia->ca", cell_potential, onehot.astype(jnp.float32), precision=lax.Precision.HIGHEST
    )
    return (window_ops, window_pot)


def local_apply(vector, window_ops, window_pot, scales):
    node_total, state_cols = vector.shape
    cell_total, width = window_pot.shape
    quarter = width // 4
    blocked = vector.reshape(cell_total, 3, quarter, state_cols)
    following = jnp.roll(blocked[:, 0], -1, axis=0)
    windows = jnp.concatenate([blocked, following[:, None]], axis=1).reshape(
        cell_total, width, state_cols
    )
    product = jnp.einsum(
        "cba,cbs->cas", window_ops, windows, preferred_element_type=jnp.float32
    )
    terms = product * scales[:, None, None] + window_pot[:, :, None] * windows.astype(jnp.float32)
    split_terms = terms.reshape(cell_total, 4, quarter, state_cols)
    first = split_terms[:, 0] + jnp.roll(split_terms[:, 3], 1, axis=0)
    folded = jnp.concatenate([first[:, None], split_terms[:, 1:3]], axis=1)
    return folded.reshape(node_total, state_cols)


def newton(gram_matrix):
    identity = jnp.eye(gram_matrix.shape[0], dtype=jnp.float32)
    frobenius = jnp.sqrt(jnp.sum(gram_matrix * gram_matrix))
    scaled = gram_matrix / frobenius
    inverse_root = identity
    for repeat in range(NS_ITERS):
        factor = 1.5 * identity - 0.5 * jnp.dot(
            inverse_root, scaled, precision=lax.Precision.HIGHEST
        )
        scaled = jnp.dot(scaled, factor, precision=lax.Precision.HIGHEST)
        inverse_root = jnp.dot(factor, inverse_root, precision=lax.Precision.HIGHEST)
    return inverse_root.astype(jnp.bfloat16)


def butterfly_sum(value):
    band_size = lax.axis_size("band")
    count = lax.axis_size("dom") * band_size
    index = lax.axis_index("dom") * band_size + lax.axis_index("band")
    bits = [b for b in range(count.bit_length() - 1)]
    order = bits[2:3] + bits[0:2] + bits[3:]
    buffer = value.reshape(-1)
    kept = []
    for bit in order:
        mask = 1 << bit
        pairs = [(i, i ^ mask) for i in range(count)]
        half = buffer.shape[0] // 2
        low, high = buffer[:half], buffer[half:]
        upper = (index & mask) != 0
        received = lax.ppermute(jnp.where(upper, low, high), ("dom", "band"), pairs)
        buffer = jnp.where(upper, high, low) + received
        kept.append((mask, upper))
    for mask, upper in reversed(kept):
        pairs = [(i, i ^ mask) for i in range(count)]
        received = lax.ppermute(buffer, ("dom", "band"), pairs)
        buffer = jnp.where(
            upper,
            jnp.concatenate([received, buffer]),
            jnp.concatenate([buffer, received]),
        )
    return buffer.reshape(value.shape)


def body(states, cell_kinetic, cell_scale, cell_potential, connectivity, shared_nodes, cell_counts):
    left_face = shared_nodes[0, 0]
    right_face = shared_nodes[0, 1]
    face_width = left_face.shape[0]
    faces = jnp.concatenate([left_face, right_face])
    live_count = cell_counts[0]
    domain = lax.axis_index("dom")
    domains = lax.axis_size("dom")
    node_total = states.shape[1]
    has_left = (domain > 0).astype(jnp.float32)
    has_right = (domain < domains - 1).astype(jnp.float32)
    multiplicity = (
        jnp.ones((node_total,), jnp.float32)
        .at[left_face]
        .add(has_left)
        .at[right_face]
        .add(has_right)
    )
    node_weight = (1.0 / multiplicity).astype(jnp.bfloat16)
    window_ops, window_pot = window_operators(
        connectivity, cell_kinetic, cell_potential, node_total
    )
    alive = (jnp.arange(window_pot.shape[0]) < live_count).astype(jnp.float32)
    scales = cell_scale * alive
    window_pot = window_pot * alive[:, None]
    up = [(i, i + 1) for i in range(domains - 1)]
    down = [(j, i) for i, j in up]

    def apply_field(vector):
        local_sum = local_apply(vector, window_ops, window_pot, scales)
        face_values = jnp.take(local_sum, faces, axis=0)
        from_left = lax.ppermute(face_values[face_width:], "dom", up)
        from_right = lax.ppermute(face_values[:face_width], "dom", down)
        received = jnp.concatenate([from_left, from_right], axis=0)
        return local_sum.at[faces].add(received, unique_indices=True)

    previous = states.T
    current = apply_field(previous).astype(jnp.bfloat16)
    for repeat in range(CHEB - 1):
        following = (2.0 * apply_field(current) - previous.astype(jnp.float32)).astype(jnp.bfloat16)
        previous = current
        current = following
    row_shard = lax.all_to_all(current, "band", split_axis=0, concat_axis=1, tiled=True)
    piece_nodes = row_shard.shape[0]
    weight_rows = lax.dynamic_slice_in_dim(
        node_weight, lax.axis_index("band") * piece_nodes, piece_nodes, 0
    )
    weighted = row_shard * weight_rows[:, None]
    partial_gram = lax.dot_general(
        weighted, row_shard, (((0,), (0,)), ((), ())), preferred_element_type=jnp.float32
    )
    gram_matrix = butterfly_sum(partial_gram)
    mixing = newton(gram_matrix)
    rotated = lax.dot_general(
        row_shard, mixing, (((1,), (0,)), ((), ())), preferred_element_type=jnp.float32
    ).astype(jnp.bfloat16)
    back = lax.all_to_all(rotated, "band", split_axis=1, concat_axis=0, tiled=True)
    return back.T


def solution(mesh):
    in_specs = (
        P("band", "dom"),
        P(),
        P("dom"),
        P("dom", None),
        P("dom", None),
        P("dom", None, None),
        P("dom"),
    )
    out_specs = P("band", "dom")
    return jax.shard_map(body, mesh=mesh, in_specs=in_specs, out_specs=out_specs, check_vma=False)
```

time: 753 us -> 572 us (0.76)
  local copies, waits for them, and re-layouts: 276 us -> 173 us
  waiting for transfers between devices: 161 us -> 78.9 us
  starting transfers between devices: 29.2 us -> 49.7 us
  between operations: 16 us -> 2.58 us
  other arithmetic: 142 us -> 153 us
    psum x1 -> x0, waiting for transfers between devices: 145 us -> none  [body(): gram_matrix = lax.psum(partial_gram, ('dom', 'band'))]
    scatter-add x8 -> x0, local copies, waits for them, and re-layouts: 133 us -> none  [local_apply(): folded = folded.at[:, :, 0].add(jnp.roll(split_terms[:, :, 3], 1, axis=1))]
    ppermute x8 -> x22, waiting for transfers between devices: 10.6 us -> 71.6 us  [the longest x7 22.6 us: butterfly_sum(): received = lax.ppermute(buffer, ('dom', 'band'), pairs)]
    concatenate x0 -> x9, local copies, waits for them, and re-layouts: none -> 27.7 us  [the longest x4 27.6 us: local_apply(): folded = jnp.concatenate([first[:, None], split_terms[:, 1:3]], axis=1)]
    ppermute x8 -> x22, starting transfers between devices: 23.9 us -> 44.4 us  [the longest x4 19.6 us: apply_field(): from_left = lax.ppermute(face_values[face_width:], 'dom', up)]
    scatter-add x8 -> x4, other arithmetic: 87.5 us -> 70 us  [apply_field(): return local_sum.at[faces].add(received, unique_indices=True)]
    concatenate x4 -> x8, other arithmetic: 13 us -> 28.6 us  [the longest x4 15.6 us: local_apply(): folded = jnp.concatenate([first[:, None], split_terms[:, 1:3]], axis=1)]
    gather x8 -> x4, local copies, waits for them, and re-layouts: 46.1 us -> 33 us  [apply_field(): face_values = jnp.take(local_sum, faces, axis=0)]
  transfers between devices with their start and end apart: 10 -> 23, of which waited for: 5 -> 23; matrix products, arithmetic and copies ran while one was open for 9% -> 2% of each run, Pallas kernels for 0% -> 0%
where the time goes in v1:
time: 572 us; the launch traced here: 566 us
  local copies, waits for them, and re-layouts  173 us (30%)
  other arithmetic  153 us (27%)
  matrix products  85.1 us (15%)
  waiting for transfers between devices  78.9 us (14%)
  starting transfers between devices  49.7 us (9%)
  blocking collectives  23.8 us (4%)
    scatter-add x4, other arithmetic, apply_field(): return local_sum.at[faces].add(received, unique_indices=True)  70 us
    dot_general x4, matrix products, local_apply(): jnp.einsum('cba,cbs->cas', window_ops, windows, preferred_element_type=jn...  42.2 us
    gather x4, local copies, waits for them, and re-layouts, apply_field(): face_values = jnp.take(local_sum, faces, axis=0)  33 us
    concatenate x4, local copies, waits for them, and re-layouts, local_apply(): folded = jnp.concatenate([first[:, None], split_terms[:, 1:3]], axis=1)  27.6 us
    all_to_all x1, blocking collectives, body(): lax.all_to_all(rotated, 'band', split_axis=1, concat_axis=0, tiled=True)  23.8 us
    ppermute x7, waiting for transfers between devices, butterfly_sum(): received = lax.ppermute(buffer, ('dom', 'band'), pairs)  22.6 us
    ppermute x7, waiting for transfers between devices, butterfly_sum(): received = lax.ppermute(jnp.where(upper, low, high), ('dom', 'band'), pairs)  22.3 us
    dot_general x1, matrix products, window_operators(): jnp.einsum('cjb,cja->cba', onehot, kinetic_cols, preferred_element_type=j...  21.6 us
  transfers between devices with their start and end apart: 23, of which 23 were waited for; matrix products, arithmetic and copies ran while one was open for 2% of the time, Pallas kernels for 0%

profile of v1, /device:TPU:6, one launch (start us, length us, event | category | flops | bytes accessed | tf_op | source)
XLA Modules:
  0.0 566.0 jit_solution(7583532414154331032)
XLA Ops:
  21.3 8.4 %iota_compare_fusion.21 = pred[32,512,512]{1,2,0:T(32,128)(4,1)} fusion(s32[32,512]{1,0:T(8,128)S(1)} %add_select_fusion), kind=kLoop, calls=%fused_computation.10.clone.1.clone.clone.clone.2 | loop fusion | flops 8388608 | bytes 8454144 | tf_op jit(solution)/shard_map/cjb,cja->cba/dot_general | solution.py:22
  29.7 15.0 %fusion = f32[32,1,512]{2,1,0:T(1,128)S(1)} fusion(s32[32,512]{1,0:T(8,128)S(1)} %add_select_fusion, f32[32,512,1]{1,0,2:T(8,128)S(1)} %bitcast.168), kind=kOutput, calls=%fused_computation.11 | convolution fusion | flops 109051904 | bytes 196608 | tf_op jit(solution)/shard_map/ci,cia->ca/dot_general | solution.py:25
  45.4 21.6 %fusion.7 = bf16[32,512,512]{2,1,0:T(8,128)(2,1)} fusion(s32[32,512]{1,0:T(8,128)S(1)} %add_select_fusion, bf16[512,512]{1,0:T(8,128)(2,1)S(1)} %copy-done, pred[32,512,512]{1,2,0:T(32,128)(4,1)} %iota_compare_fusion.21), kind=kOutput, calls=%fused_computation.17 | convolution fusion | flops 17205035008 | bytes 25755648 | tf_op jit(solution)/shard_map/cjb,cja->cba/dot_general | solution.py:22
  67.0 10.5 %multiply_add_fusion.3 = f32[32,512,64]{1,2,0:T(8,128)} fusion(bf16[32,512,64]{1,2,0:T(8,128)(2,1)S(1)} %reshape.276, bf16[32,512,512]{2,1,0:T(8,128)(2,1)} %fusion.7, f32[32,512]{1,0:T(8,128)S(1)} %bitcast_multiply_fusion.1, f32[32]{0:T(128)S(1)} %compare_select_fusion.4), kind=kOutput, calls=%fused_computation.28 | convolution fusion | flops 1077936128 | bytes 23134336 | tf_op jit(solution)/shard_map/cba,cbs->cas/dot_general | solution.py:40
  77.5 5.7 %reshape.277 = f32[32,4,128,64]{2,1,3,0:T(4,128)} reshape(f32[32,512,64]{1,2,0:T(8,128)} %multiply_add_fusion.3) | data formatting | bytes 8388608 | tf_op jit(solution)/shard_map/reshape | solution.py:44
  98.0 6.9 %copy.54 = f32[32,3,128,64]{3,2,1,0:T(8,128)} copy(f32[32,3,128,64]{2,1,3,0:T(4,128)} %pad_maximum_fusion) | data formatting | bytes 6291456 | tf_op jit(solution)/shard_map/concatenate | solution.py:46
  104.9 8.2 %gather_fusion = f32[2048,64]{1,0:T(8,128)S(1)} fusion(f32[12288,64]{1,0:T(8,128)} %bitcast.122, s32[2048]{0:T(1024)S(1)} %fusion.39), kind=kCustom, calls=%fused_computation.clone | custom fusion | bytes 1056768 | tf_op jit(solution)/shard_map/jit(_take)/gather | solution.py:122
  125.9 17.4 %scatter_custom_fusion = f32[12288,64]{1,0:T(8,128)} fusion(f32[12288,64]{1,0:T(8,128)} %bitcast.123, s32[2048]{0:T(1024)S(1)} %bitcast.163, f32[1024,64]{1,0:T(8,128)S(1)} %collective-permute-done.1, f32[]{:T(128)} %constant.70, f32[1024,64]{1,0:T(8,128)S(1)} %collective-permute-done), kind=kCustom, calls=%fused_computation.50 | custom fusion | flops 262144 | bytes 4194816 | tf_op jit(solution)/shard_map/scatter-add | solution.py:126
  162.3 10.6 %multiply_add_fusion.2 = f32[32,512,64]{1,2,0:T(8,128)} fusion(bf16[32,512,64]{1,2,0:T(8,128)(2,1)S(1)} %reshape.280, bf16[32,512,512]{2,1,0:T(8,128)(2,1)} %fusion.7, f32[32,512]{1,0:T(8,128)S(1)} %bitcast_multiply_fusion.1, f32[32]{0:T(128)S(1)} %compare_select_fusion.4), kind=kOutput, calls=%fused_computation.27 | convolution fusion | flops 1077936128 | bytes 23134336 | tf_op jit(solution)/shard_map/cba,cbs->cas/dot_general | solution.py:40
  172.9 5.2 reshape.281
  192.8 6.9 %copy.59 = f32[32,3,128,64]{3,2,1,0:T(8,128)} copy(f32[32,3,128,64]{2,1,3,0:T(4,128)} %pad_maximum_fusion.1) | data formatting | bytes 6291456 | tf_op jit(solution)/shard_map/concatenate | solution.py:46
  199.7 8.2 %gather_fusion.1 = f32[2048,64]{1,0:T(8,128)S(1)} fusion(f32[12288,64]{1,0:T(8,128)} %bitcast.126, s32[2048]{0:T(1024)S(1)} %fusion.39), kind=kCustom, calls=%fused_computation.1.clone | custom fusion | bytes 1056768 | tf_op jit(solution)/shard_map/jit(_take)/gather | solution.py:122
  208.3 5.8 %collective-permute-start.2 = (f32[1024,64]{1,0:T(8,128)S(1)}, f32[1024,64]{1,0:T(8,128)S(1)}, u32[]{:S(2)}, u32[]{:S(2)}) collective-permute-start(f32[1024,64]{1,0:T(8,128)S(1)} %get-tuple-element.10), channel_id=1, source_target_pairs={{0,4},{4,8},{8,12},{12,16},{16,20},{20,24},{24,28},{28,32},{32,36}... | collective-permute-start | bytes 786440 | tf_op jit(solution)/shard_map/ppermute | solution.py:123
  222.7 17.4 %scatter_custom_fusion.1 = f32[12288,64]{1,0:T(8,128)} fusion(f32[12288,64]{1,0:T(8,128)} %bitcast.127, s32[2048]{0:T(1024)S(1)} %bitcast.164, f32[1024,64]{1,0:T(8,128)S(1)} %collective-permute-done.3, f32[]{:T(128)} %constant.70, f32[1024,64]{1,0:T(8,128)S(1)} %collective-permute-done.2), kind=kCustom, calls=%fused_computation.54 | custom fusion | flops 262144 | bytes 4194816 | tf_op jit(solution)/shard_map/scatter-add | solution.py:126
  260.5 10.6 %multiply_add_fusion.1 = f32[32,512,64]{1,2,0:T(8,128)} fusion(bf16[32,512,64]{1,2,0:T(8,128)(2,1)S(1)} %reshape.284, bf16[32,512,512]{2,1,0:T(8,128)(2,1)} %fusion.7, f32[32,512]{1,0:T(8,128)S(1)} %bitcast_multiply_fusion.1, f32[32]{0:T(128)S(1)} %compare_select_fusion.4), kind=kOutput, calls=%fused_computation.26 | convolution fusion | flops 1077936128 | bytes 23134336 | tf_op jit(solution)/shard_map/cba,cbs->cas/dot_general | solution.py:40
  271.0 5.2 reshape.285
  290.9 6.9 %copy.64 = f32[32,3,128,64]{3,2,1,0:T(8,128)} copy(f32[32,3,128,64]{2,1,3,0:T(4,128)} %pad_maximum_fusion.2) | data formatting | bytes 6291456 | tf_op jit(solution)/shard_map/concatenate | solution.py:46
  297.8 8.2 %gather_fusion.2 = f32[2048,64]{1,0:T(8,128)S(1)} fusion(f32[12288,64]{1,0:T(8,128)} %bitcast.128, s32[2048]{0:T(1024)S(1)} %fusion.39), kind=kCustom, calls=%fused_computation.2.clone | custom fusion | bytes 1056768 | tf_op jit(solution)/shard_map/jit(_take)/gather | solution.py:122
  306.5 5.9 %collective-permute-start.4 = (f32[1024,64]{1,0:T(8,128)S(1)}, f32[1024,64]{1,0:T(8,128)S(1)}, u32[]{:S(2)}, u32[]{:S(2)}) collective-permute-start(f32[1024,64]{1,0:T(8,128)S(1)} %get-tuple-element.8), channel_id=1, source_target_pairs={{0,4},{4,8},{8,12},{12,16},{16,20},{20,24},{24,28},{28,32},{32,36}... | collective-permute-start | bytes 786440 | tf_op jit(solution)/shard_map/ppermute | solution.py:123
  321.0 17.5 %scatter_custom_fusion.2 = f32[12288,64]{1,0:T(8,128)} fusion(f32[12288,64]{1,0:T(8,128)} %bitcast.129, s32[2048]{0:T(1024)S(1)} %bitcast.165, f32[1024,64]{1,0:T(8,128)S(1)} %collective-permute-done.5, f32[]{:T(128)} %constant.70, f32[1024,64]{1,0:T(8,128)S(1)} %collective-permute-done.4), kind=kCustom, calls=%fused_computation.58 | custom fusion | flops 262144 | bytes 4194816 | tf_op jit(solution)/shard_map/scatter-add | solution.py:126
  359.3 10.5 %multiply_add_fusion = f32[32,512,64]{1,2,0:T(8,128)} fusion(bf16[32,512,64]{1,2,0:T(8,128)(2,1)S(1)} %reshape.288, bf16[32,512,512]{2,1,0:T(8,128)(2,1)} %fusion.7, f32[32,512]{1,0:T(8,128)S(1)} %bitcast_multiply_fusion.1, f32[32]{0:T(128)S(1)} %compare_select_fusion.4), kind=kOutput, calls=%fused_computation.25 | convolution fusion | flops 1077936128 | bytes 23134336 | tf_op jit(solution)/shard_map/cba,cbs->cas/dot_general | solution.py:40
  369.8 5.2 reshape.289
  389.8 6.9 %copy.69 = f32[32,3,128,64]{3,2,1,0:T(8,128)} copy(f32[32,3,128,64]{2,1,3,0:T(4,128)} %pad_maximum_fusion.3) | data formatting | bytes 6291456 | tf_op jit(solution)/shard_map/concatenate | solution.py:46
  396.7 8.2 %gather_fusion.3 = f32[2048,64]{1,0:T(8,128)S(1)} fusion(f32[12288,64]{1,0:T(8,128)} %bitcast.124, s32[2048]{0:T(1024)S(1)} %fusion.39), kind=kCustom, calls=%fused_computation.3.clone | custom fusion | bytes 1056768 | tf_op jit(solution)/shard_map/jit(_take)/gather | solution.py:122
  405.3 5.9 %collective-permute-start.6 = (f32[1024,64]{1,0:T(8,128)S(1)}, f32[1024,64]{1,0:T(8,128)S(1)}, u32[]{:S(2)}, u32[]{:S(2)}) collective-permute-start(f32[1024,64]{1,0:T(8,128)S(1)} %get-tuple-element.6), channel_id=1, source_target_pairs={{0,4},{4,8},{8,12},{12,16},{16,20},{20,24},{24,28},{28,32},{32,36}... | collective-permute-start | bytes 786440 | tf_op jit(solution)/shard_map/ppermute | solution.py:123
  419.9 17.6 %scatter_custom_fusion.3 = f32[12288,64]{1,0:T(8,128)} fusion(f32[12288,64]{1,0:T(8,128)} %bitcast.125, s32[2048]{0:T(1024)S(1)} %bitcast.166, f32[1024,64]{1,0:T(8,128)S(1)} %collective-permute-done.7, f32[]{:T(128)} %constant.70, f32[1024,64]{1,0:T(8,128)S(1)} %collective-permute-done.6), kind=kCustom, calls=%fused_computation.62 | custom fusion | flops 262144 | bytes 4194816 | tf_op jit(solution)/shard_map/scatter-add | solution.py:126
  437.5 5.4 subtract_convert_fusion
  447.2 5.3 all-to-all-start
  452.5 5.9 %scatter_custom_fusion.4 = f32[12288]{0:T(1024)S(1)} fusion(s32[1024]{0:T(1024)S(1)} %bitcast.167, f32[1024]{0:T(1024)S(1)} %broadcast.110, f32[]{:T(128)} %constant.25.clone.1), kind=kCustom, calls=%fused_computation.97 | custom fusion | flops 1024 | bytes 49156 | tf_op jit(solution)/shard_map/scatter-add | solution.py:106
  458.5 6.1 %scatter_fusion = f32[12288]{0:T(1024)S(1)} fusion(f32[12288]{0:T(1024)S(1)} %scatter_custom_fusion.4, s32[1024]{0:T(1024)S(1)} %bitcast.162, f32[1024]{0:T(1024)S(1)} %broadcast.111), kind=kCustom, calls=%fused_computation.9 | custom fusion | flops 1024 | bytes 16384 | tf_op jit(solution)/shard_map/scatter-add | solution.py:108
  464.6 7.3 %all-to-all-done = bf16[4,3072,64]{1,2,0:T(8,128)(2,1)S(1)} async-done(((bf16[4,3072,64]{1,2,0:T(8,128)(2,1)}), bf16[4,3072,64]{1,2,0:T(8,128)(2,1)S(1)}, u32[]{:S(2)}, u32[]{:S(2)}) %all-to-all-start) | async-done | bytes 1572896 | tf_op jit(solution)/shard_map/all_to_all | solution.py:134
  540.8 23.8 %all_to_all.38 = bf16[3072,4,64]{0,2,1:T(8,128)(2,1)S(1)} all-to-all(bf16[3072,4,64]{0,2,1:T(8,128)(2,1)S(1)} %bitcast.145), channel_id=1, replica_groups=mesh['dom'=32,'band'=4] {'band'}, dimensions={1} | all-to-all | bytes 3145728 | tf_op jit(solution)/shard_map/all_to_all | solution.py:148
  (190 shorter events, 253.0 us)
Async XLA Ops:
  0.0 45.4 %copy-start = (bf16[512,512]{1,0:T(8,128)(2,1)S(1)}, bf16[512,512]{1,0:T(8,128)(2,1)}, u32[]{:S(2)}) copy-start(bf16[512,512]{1,0:T(8,128)(2,1)} %param.10) | copy-start | bytes 1572868
  15.0 6.2 %copy-start.5 = (s32[32,512]{1,0:T(8,128)S(1)}, s32[32,512]{1,0:T(8,128)}, u32[]{:S(2)}) copy-start(s32[32,512]{1,0:T(8,128)} %param.13) | copy-start | bytes 196612
  21.3 8.4 %copy-start.7 = (f32[32,512]{1,0:T(8,128)S(1)}, f32[32,512]{1,0:T(8,128)}, u32[]{:S(2)}) copy-start(f32[32,512]{1,0:T(8,128)} %param.12) | copy-start | bytes 196612
  45.4 21.7 %copy-start.8 = (f32[32]{0:T(128)S(1)}, f32[32]{0:T(128)}, u32[]{:S(2)}) copy-start(f32[32]{0:T(128)} %param.11) | copy-start | bytes 388
  83.2 7.5 %copy-start.6 = (s32[1,2,1024]{2,1,0:T(2,128)S(1)}, s32[1,2,1024]{2,1,0:T(2,128)}, u32[]{:S(2)}) copy-start(s32[1,2,1024]{2,1,0:T(2,128)} %param.14) | copy-start | bytes 24580
  113.6 10.5 %collective-permute-start = (f32[1024,64]{1,0:T(8,128)S(1)}, f32[1024,64]{1,0:T(8,128)S(1)}, u32[]{:S(2)}, u32[]{:S(2)}) collective-permute-start(f32[1024,64]{1,0:T(8,128)S(1)} %get-tuple-element.12), channel_id=1, source_target_pairs={{0,4},{4,8},{8,12},{12,16},{16,20},{20,24},{24,28},{28,32},{32,36}... | collective-permute-start | bytes 786440 | tf_op jit(solution)/shard_map/ppermute | solution.py:123
  115.5 10.3 %collective-permute-start.1 = (f32[1024,64]{1,0:T(8,128)S(1)}, f32[1024,64]{1,0:T(8,128)S(1)}, u32[]{:S(2)}, u32[]{:S(2)}) collective-permute-start(f32[1024,64]{1,0:T(8,128)S(1)} %get-tuple-element.13), channel_id=1, source_target_pairs={{4,0},{8,4},{12,8},{16,12},{20,16},{24,20},{28,24},{32,28},{36,32}... | collective-permute-start | bytes 786440 | tf_op jit(solution)/shard_map/ppermute | solution.py:124
  146.5 2.0 copy-start.3
  208.3 10.7 %collective-permute-start.2 = (f32[1024,64]{1,0:T(8,128)S(1)}, f32[1024,64]{1,0:T(8,128)S(1)}, u32[]{:S(2)}, u32[]{:S(2)}) collective-permute-start(f32[1024,64]{1,0:T(8,128)S(1)} %get-tuple-element.10), channel_id=1, source_target_pairs={{0,4},{4,8},{8,12},{12,16},{16,20},{20,24},{24,28},{28,32},{32,36}... | collective-permute-start | bytes 786440 | tf_op jit(solution)/shard_map/ppermute | solution.py:123
  214.1 8.6 %collective-permute-start.3 = (f32[1024,64]{1,0:T(8,128)S(1)}, f32[1024,64]{1,0:T(8,128)S(1)}, u32[]{:S(2)}, u32[]{:S(2)}) collective-permute-start(f32[1024,64]{1,0:T(8,128)S(1)} %get-tuple-element.11), channel_id=1, source_target_pairs={{4,0},{8,4},{12,8},{16,12},{20,16},{24,20},{28,24},{32,28},{36,32}... | collective-permute-start | bytes 786440 | tf_op jit(solution)/shard_map/ppermute | solution.py:124
  244.7 1.9 copy-start.2
  306.5 10.7 %collective-permute-start.4 = (f32[1024,64]{1,0:T(8,128)S(1)}, f32[1024,64]{1,0:T(8,128)S(1)}, u32[]{:S(2)}, u32[]{:S(2)}) collective-permute-start(f32[1024,64]{1,0:T(8,128)S(1)} %get-tuple-element.8), channel_id=1, source_target_pairs={{0,4},{4,8},{8,12},{12,16},{16,20},{20,24},{24,28},{28,32},{32,36}... | collective-permute-start | bytes 786440 | tf_op jit(solution)/shard_map/ppermute | solution.py:123
  312.4 8.6 %collective-permute-start.5 = (f32[1024,64]{1,0:T(8,128)S(1)}, f32[1024,64]{1,0:T(8,128)S(1)}, u32[]{:S(2)}, u32[]{:S(2)}) collective-permute-start(f32[1024,64]{1,0:T(8,128)S(1)} %get-tuple-element.9), channel_id=1, source_target_pairs={{4,0},{8,4},{12,8},{16,12},{20,16},{24,20},{28,24},{32,28},{36,32}... | collective-permute-start | bytes 786440 | tf_op jit(solution)/shard_map/ppermute | solution.py:124
  343.6 2.0 copy-start.4
  405.3 10.7 %collective-permute-start.6 = (f32[1024,64]{1,0:T(8,128)S(1)}, f32[1024,64]{1,0:T(8,128)S(1)}, u32[]{:S(2)}, u32[]{:S(2)}) collective-permute-start(f32[1024,64]{1,0:T(8,128)S(1)} %get-tuple-element.6), channel_id=1, source_target_pairs={{0,4},{4,8},{8,12},{12,16},{16,20},{20,24},{24,28},{28,32},{32,36}... | collective-permute-start | bytes 786440 | tf_op jit(solution)/shard_map/ppermute | solution.py:123
  411.3 8.6 %collective-permute-start.7 = (f32[1024,64]{1,0:T(8,128)S(1)}, f32[1024,64]{1,0:T(8,128)S(1)}, u32[]{:S(2)}, u32[]{:S(2)}) collective-permute-start(f32[1024,64]{1,0:T(8,128)S(1)} %get-tuple-element.7), channel_id=1, source_target_pairs={{4,0},{8,4},{12,8},{16,12},{20,16},{24,20},{28,24},{32,28},{36,32}... | collective-permute-start | bytes 786440 | tf_op jit(solution)/shard_map/ppermute | solution.py:124
  447.2 24.7 %all-to-all-start = ((bf16[4,3072,64]{1,2,0:T(8,128)(2,1)}), bf16[4,3072,64]{1,2,0:T(8,128)(2,1)S(1)}, u32[]{:S(2)}, u32[]{:S(2)}) async-start(bf16[4,3072,64]{1,2,0:T(8,128)(2,1)} %copy.70), calls=%async_computation | async-start | bytes 3145728 | tf_op jit(solution)/shard_map/all_to_all | solution.py:134
  472.7 3.7 collective-permute-start.8
  476.4 4.4 collective-permute-start.9
  480.9 5.5 collective-permute-start.10
  486.4 3.8 collective-permute-start.11
  490.2 5.2 collective-permute-start.12
  495.5 3.7 collective-permute-start.13
  499.2 5.2 collective-permute-start.14
  504.3 5.1 collective-permute-start.15
  509.4 3.6 collective-permute-start.16
  513.1 5.2 collective-permute-start.17
  518.2 3.7 collective-permute-start.18
  522.0 5.4 collective-permute-start.19
  527.4 4.3 collective-permute-start.20
  531.8 1.7 collective-permute-start.21
  539.7 26.1 %copy-start.1 = (bf16[512,512]{1,0:T(8,128)(2,1)S(1)}, bf16[512,512]{1,0:T(8,128)(2,1)}, u32[]{:S(2)}) copy-start(bf16[512,512]{1,0:T(8,128)(2,1)} %param.10) | copy-start | bytes 1572868
